TPU v7x, 32 devices: a whole 2x2x4 slice. The times are simulated.
32 devices in a mesh: grp: 2 (over y), gx: 16 (over z, x, core).
Axes of the slice: x: 2, y: 2, z: 4, core: 2. Of those that a mesh axis runs over, the one named last changes fastest.
Arguments:
- volume: float32 [512, 896], P(('grp', 'gx')), parts along dimension 0, may hold values from -45 to 45
- bank: float32 [8, 4096], P(None, 'gx'), may hold values from -43 to 43
- orient: int32 [8], replicated, may hold values from 0 to 47
- bank_id: int32 [8], replicated, may hold values from 0 to 7, each once
- counts: int32 [8], replicated, may hold values from 1 to 16
Outputs:
- fields: float32 [4, 512, 896], P(None, ('grp', 'gx')), parts along dimension 1
There are 2 independent parts, one for each index of `grp`. A program takes and returns all parts, laid end to end along the dimension named above; an argument that names none is the same for every part. Nothing has to cross between parts.
Inputs may be any that keep to these rules, and one draw needn't show every extreme that they name: `bank_id`: each of the 8 base templates is named by exactly one list entry.
All inputs are finite; a program needn't handle non-finite values.
Results may differ from a plain program's by a relative error of at most 0.0003.
Values sent between devices are 32-bit elements; how exact they have to be, the bound alone decides.
No kernel may reach another device: no remote copies, remote signals or barrier semaphores. Data moves between devices by JAX's collectives and lax.ppermute only.
A program may use at most 64 MiB of HBM per device.

v0:
```python
import math
import jax
import jax.numpy as jnp
import numpy as np
from jax import lax
from jax.sharding import PartitionSpec as P

BY = 8
BZ = 112
TS = 16
NT = 8
FIELDS = 4
epsilon = 1e-05
sharpness = 80.0
AXIS_ORDERS = np.array([[0, 1, 2], [0, 2, 1], [1, 0, 2], [1, 2, 0], [2, 0, 1], [2, 1, 0]], np.int32)


def extended(x, sides, width):
    for axis, dim in sides:
        size, length = (lax.axis_size(axis), x.shape[dim])
        up = [(i, (i + 1) % size) for i in range(size - 1)]
        down = [(j, i) for i, j in up]
        last = lax.slice_in_dim(x, length - width, length, axis=dim)
        leading = lax.slice_in_dim(x, 0, width, axis=dim)
        before = lax.ppermute(last, axis, up)
        after = lax.ppermute(leading, axis, down)
        x = jnp.concatenate([before, x, after], axis=dim)
    return x


def padded_length(length):
    return -(-length // 128) * 128


def rotate_template(flat_base, orient_one):
    coords = jnp.arange(TS**3, dtype=jnp.int32)
    index_set = jnp.stack([coords // (TS * TS), coords // TS % TS, coords % TS])
    order_row = orient_one // 8
    flip_set = orient_one % 8
    picked = (jnp.arange(6, dtype=jnp.int32) == order_row).astype(jnp.int32)
    ordering = jnp.sum(picked[:, None] * jnp.asarray(AXIS_ORDERS), axis=0)
    source = jnp.zeros_like(coords)
    for axis_num in range(3):
        select = (ordering[axis_num] == jnp.arange(3, dtype=jnp.int32)).astype(jnp.int32)
        chosen = jnp.sum(select[:, None] * index_set, axis=0)
        flipped = flip_set // 2**axis_num % 2
        placed = chosen + flipped * (TS - 1 - 2 * chosen)
        source = source * TS + placed
    return flat_base[source]


def normalized_kernel(flat_base, orient_one):
    rotated = rotate_template(flat_base, orient_one)
    centered = rotated - jnp.mean(rotated)
    return centered / jnp.sqrt(jnp.sum(centered * centered) + epsilon)


def wave_tables(positions, targets, period, direction):
    turns = (positions[:, None] * targets[None, :] % period).astype(jnp.float32)
    phase = 2.0 * math.pi / period * turns
    return (jnp.cos(phase), direction * jnp.sin(phase))


def band_table(positions, targets, period):
    offset = (positions[:, None] - targets[None, :]) % period
    return (offset < TS).astype(jnp.float32)


def contract(letters, data, table):
    return jnp.einsum(letters, data, table, precision=lax.Precision.HIGHEST)


def spectrum_along(real_part, imag_part, cos_table, sin_table, letters):
    new_real = contract(letters, real_part, cos_table) - contract(letters, imag_part, sin_table)
    new_imag = contract(letters, real_part, sin_table) + contract(letters, imag_part, cos_table)
    return (new_real, new_imag)


def local(volume, bank, orient, bank_id, counts):
    rows_x = volume.shape[0]
    half = TS // 2
    grid = volume.reshape(rows_x, BY, BZ)
    len_x = rows_x + TS
    len_y = BY + TS
    len_z = padded_length(BZ + TS)
    gathered = lax.all_gather(bank, "gx", axis=1, tiled=True)
    kernels = jax.vmap(normalized_kernel)(gathered[bank_id], orient)
    field_in = extended(grid, (("gx", 0),), half)
    pos_x = jnp.arange(len_x, dtype=jnp.int32)
    out_x = jnp.arange(rows_x, dtype=jnp.int32)
    pos_y = half + jnp.arange(BY, dtype=jnp.int32)
    pos_z = half + jnp.arange(BZ, dtype=jnp.int32)
    freq_x = jnp.arange(len_x, dtype=jnp.int32)
    freq_y = jnp.arange(len_y, dtype=jnp.int32)
    freq_z = jnp.arange(len_z, dtype=jnp.int32)
    tmpl_pos = jnp.arange(TS, dtype=jnp.int32)
    cos_z, sin_z = wave_tables(pos_z, freq_z, len_z, -1.0)
    cos_y, sin_y = wave_tables(pos_y, freq_y, len_y, -1.0)
    cos_x, sin_x = wave_tables(pos_x, freq_x, len_x, -1.0)
    vol_re = contract("xyz,zk->xyk", field_in, cos_z)
    vol_im = contract("xyz,zk->xyk", field_in, sin_z)
    vol_re, vol_im = spectrum_along(vol_re, vol_im, cos_y, sin_y, "xyk,yj->xjk")
    vol_re, vol_im = spectrum_along(vol_re, vol_im, cos_x, sin_x, "xjk,xi->ijk")
    kcos_z, ksin_z = wave_tables(tmpl_pos, freq_z, len_z, -1.0)
    kcos_y, ksin_y = wave_tables(tmpl_pos, freq_y, len_y, -1.0)
    kcos_x, ksin_x = wave_tables(tmpl_pos, freq_x, len_x, -1.0)
    icos_y, isin_y = wave_tables(freq_y, jnp.arange(BY, dtype=jnp.int32), len_y, 1.0)
    icos_x, isin_x = wave_tables(freq_x, out_x, len_x, 1.0)
    icos_z, isin_z = wave_tables(freq_z, jnp.arange(BZ, dtype=jnp.int32), len_z, 1.0)
    inverse_scale = 1.0 / (len_x * len_y * len_z)

    def correlate(kernel_flat):
        kernel = kernel_flat.reshape(TS, TS, TS)
        kernel_re = contract("xyz,zk->xyk", kernel, kcos_z)
        kernel_im = contract("xyz,zk->xyk", kernel, ksin_z)
        kernel_re, kernel_im = spectrum_along(kernel_re, kernel_im, kcos_y, ksin_y, "xyk,yj->xjk")
        kernel_re, kernel_im = spectrum_along(kernel_re, kernel_im, kcos_x, ksin_x, "xjk,xi->ijk")
        prod_re = kernel_re * vol_re + kernel_im * vol_im
        prod_im = kernel_re * vol_im - kernel_im * vol_re
        prod_re, prod_im = spectrum_along(prod_re, prod_im, icos_y, isin_y, "ijk,jn->ink")
        prod_re, prod_im = spectrum_along(prod_re, prod_im, icos_x, isin_x, "ink,im->mnk")
        real_out = contract("mnk,kz->mnz", prod_re, icos_z) - contract(
            "mnk,kz->mnz", prod_im, isin_z
        )
        return real_out * inverse_scale

    numer = lax.map(correlate, kernels)
    squares = field_in * field_in
    energy = contract(
        "xyz,zn->xyn", squares, band_table(pos_z, jnp.arange(BZ, dtype=jnp.int32), len_z)
    )
    energy = contract(
        "xyn,ym->xmn", energy, band_table(pos_y, jnp.arange(BY, dtype=jnp.int32), len_y)
    )
    energy = contract("xmn,xl->lmn", energy, band_table(pos_x, out_x, len_x))
    scores = numer / jnp.sqrt(energy + epsilon)[None]
    weights = counts.astype(jnp.float32)
    weighted = weights[:, None, None, None] * jnp.exp(sharpness * scores)
    grouped = jnp.sum(weighted.reshape(FIELDS, NT // FIELDS, rows_x, BY, BZ), axis=1)
    totals = jnp.sum(weights.reshape(FIELDS, NT // FIELDS), axis=1)
    fields = jnp.log(grouped / totals[:, None, None, None])
    return fields.reshape(FIELDS, rows_x, BY * BZ)


def solution(mesh):
    in_specs = (P(("grp", "gx"), None), P(None, "gx"), P(), P(), P())
    out_specs = P(None, ("grp", "gx"), None)
    return jax.shard_map(local, mesh=mesh, in_specs=in_specs, out_specs=out_specs, check_vma=False)
```

profile of v0, /device:TPU:0, one launch (start us, length us, event | category | flops | bytes accessed | tf_op | source)
XLA Modules:
  0.0 316.0 jit_solution(17705312637097414959)
XLA Ops:
  0.0 0.8 fusion.433
  0.8 2.3 collective-permute-start
  3.3 1.3 collective-permute-start.1
  4.6 0.7 compare_select_fusion.3
  5.3 0.7 and_select_fusion.8
  6.1 0.8 multiply_reduce_fusion.4
  6.9 25.6 %all_gather.3 = f32[8,4096]{1,0:T(8,128)S(1)} all-gather(f32[8,256]{1,0:T(8,128)} %param.9), channel_id=1, replica_groups=mesh['grp'=2,'gx'=16] {'gx'}, dimensions={1}, use_global_device_ids=true | all-gather | bytes 139264 | tf_op jit(solution)/shard_map/all_gather | solution.py:86
  32.9 0.6 gather_fusion
  33.5 200.1 %gather_fusion.1 = f32[32768]{0:T(1024)S(1)} fusion(f32[8,4096]{1,0:T(8,128)S(1)} %gather_fusion, s32[32768]{0:T(1024)S(1)} %bitcast.250), kind=kCustom, calls=%fused_computation.1 | custom fusion | bytes 524288 | tf_op jit(solution)/shard_map/vmap()/gather | solution.py:49
  235.9 0.6 fusion.332
  236.6 0.6 fusion.336
  237.2 0.6 fusion.250
  239.8 0.6 fusion.249
  240.5 0.6 convolution_subtract_fusion.5
  241.0 0.6 convolution_add_fusion.4
  241.6 73.3 %while.12 = (s32[]{:T(128)}, f32[8,16,8,112]{3,2,1,0:T(8,128)S(1)}, f32[8,4096]{1,0:T(8,128)S(1)}, f32[32,24,128]{2,0,1:T(8,128)S(1)}, f32[32,24,128]{2,0,1:T(8,128)S(1)}, /*index=5*/s32[]{:T(128)}) while((s32[]{:T(128)}, f32[8,16,8,112]{3,2,1,0:T(8,128)S(1)}, f32[8,4096]{1,0:T(8,128)S(1)}, ...), condition=%wide.region_7.8_spmd.clone.clone, body=%wide.region_6.7_spmd.clone.clone.sunk | while | flops 234336256 | bytes 10379349 | solution.py:127
  245.4 0.6 fusion.548
  246.0 0.7 multiply_subtract_fusion.2
  254.6 0.6 fusion.548
  255.1 0.7 multiply_subtract_fusion.2
  263.7 0.6 fusion.548
  264.3 0.7 multiply_subtract_fusion.2
  272.8 0.6 fusion.548
  273.4 0.7 multiply_subtract_fusion.2
  282.0 0.6 fusion.548
  282.5 0.7 multiply_subtract_fusion.2
  291.1 0.6 fusion.548
  291.7 0.7 multiply_subtract_fusion.2
  300.2 0.6 fusion.548
  300.8 0.7 multiply_subtract_fusion.2
  310.0 0.7 multiply_subtract_fusion.2
  315.2 0.8 divide_log_fusion
  (208 shorter events, 67.2 us)
Async XLA Ops:
  0.8 233.9 %collective-permute-start = (f32[8,8,112]{2,1,0:T(8,128)S(1)}, f32[8,8,112]{2,1,0:T(8,128)S(1)}, u32[]{:S(2)}, u32[]{:S(2)}) collective-permute-start(f32[8,8,112]{2,1,0:T(8,128)S(1)} %slice.34), channel_id=1, source_target_pairs={{0,1},{1,2},{2,3},{3,4},{4,5},{5,6},{6,7},{7,8},{8,9},{9,10},{10,1... | collective-permute-start | bytes 86024 | tf_op jit(solution)/shard_map/ppermute | solution.py:25
  3.3 231.5 %collective-permute-start.1 = (f32[8,8,112]{2,1,0:T(8,128)S(1)}, f32[8,8,112]{2,1,0:T(8,128)S(1)}, u32[]{:S(2)}, u32[]{:S(2)}) collective-permute-start(f32[8,8,112]{2,1,0:T(8,128)S(1)} %slice.36), channel_id=1, source_target_pairs={{1,0},{2,1},{3,2},{4,3},{5,4},{6,5},{7,6},{8,7},{9,8},{10,9},{11,1... | collective-permute-start | bytes 86024 | tf_op jit(solution)/shard_map/ppermute | solution.py:26
  233.6 0.8 copy-start
  233.6 0.9 copy-start.1
where the time goes:
time: 316 us
  local copies, waits for them, and re-layouts  203 us (64%)
  matrix products  77.2 us (24%)
  blocking collectives  25.6 us (8%)
  other arithmetic  4.22 us (1%)
  starting transfers between devices  3.63 us (1%)
    gather x2, local copies, waits for them, and re-layouts, rotate_template(): return flat_base[source]  200 us
    dot_general x173, matrix products, contract(): return jnp.einsum(letters, data, table, precision=lax.Precision.HIGHEST)  77.2 us
    all_gather x1, blocking collectives, local(): gathered = lax.all_gather(bank, 'gx', axis=1, tiled=True)  25.6 us
  transfers between devices with their start and end apart: 2, of which 0 were waited for; matrix products, arithmetic and copies ran while one was open for 65% of the time, Pallas kernels for 0%

commit v1 on v0

--- a/solution.py
+++ b/solution.py
@@ -83,7 +83,16 @@
     len_x = rows_x + TS
     len_y = BY + TS
     len_z = padded_length(BZ + TS)
-    gathered = lax.all_gather(bank, "gx", axis=1, tiled=True)
+    count, index, span = (lax.axis_size("gx"), lax.axis_index("gx"), bank.shape[1])
+    right = [(i_2, (i_2 + 1) % count) for i_2 in range(count)]
+    out = jnp.zeros((*bank.shape[:1], count * span, *bank.shape[1 + 1 :]), bank.dtype)
+    held = bank
+    for step in range(count):
+        owner = (index - step) % count
+        out = lax.dynamic_update_slice_in_dim(out, held, owner * span, axis=1)
+        if step < count - 1:
+            held = lax.ppermute(held, "gx", right)
+    gathered = out
     kernels = jax.vmap(normalized_kernel)(gathered[bank_id], orient)
     field_in = extended(grid, (("gx", 0),), half)
     pos_x = jnp.arange(len_x, dtype=jnp.int32)

time: 316 us -> 368 us (1.16)
  waiting for transfers between devices: 0.01 us -> 73.9 us
  blocking collectives: 25.6 us -> 0 us
  starting transfers between devices: 3.63 us -> 7.5 us
    ppermute x0 -> x15, waiting for transfers between devices: none -> 73.9 us  [local(): held = lax.ppermute(held, 'gx', right)]
    all_gather x1 -> x0, blocking collectives: 25.6 us -> none  [local(): gathered = lax.all_gather(bank, 'gx', axis=1, tiled=True)]
  transfers between devices with their start and end apart: 2 -> 17, of which waited for: 0 -> 13; matrix products, arithmetic and copies ran while one was open for 65% -> 3% of each run, Pallas kernels for 0% -> 0%
where the time goes in v1:
time: 368 us
  local copies, waits for them, and re-layouts  203 us (55%)
  matrix products  77.2 us (21%)
  waiting for transfers between devices  73.9 us (20%)
  starting transfers between devices  7.5 us (2%)
    gather x2, local copies, waits for them, and re-layouts, rotate_template(): return flat_base[source]  200 us
    dot_general x173, matrix products, contract(): return jnp.einsum(letters, data, table, precision=lax.Precision.HIGHEST)  77.2 us
    ppermute x15, waiting for transfers between devices, local(): held = lax.ppermute(held, 'gx', right)  73.9 us
  transfers between devices with their start and end apart: 17, of which 13 were waited for; matrix products, arithmetic and copies ran while one was open for 3% of the time, Pallas kernels for 0%

profile of v1, /device:TPU:0, one launch (start us, length us, event | category | flops | bytes accessed | tf_op | source)
XLA Modules:
  0.0 367.8 jit_solution(6596251827792492727)
XLA Ops:
  0.5 0.8 fusion.428
  1.3 4.5 %collective-permute-start.15 = (f32[8,8,112]{2,1,0:T(8,128)S(1)}, f32[8,8,112]{2,1,0:T(8,128)S(1)}, u32[]{:S(2)}, u32[]{:S(2)}) collective-permute-start(f32[8,8,112]{2,1,0:T(8,128)S(1)} %slice.34), channel_id=1, source_target_pairs={{0,1},{1,2},{2,3},{3,4},{4,5},{5,6},{6,7},{7,8},{8,9},{9,10},{10,1... | collective-permute-start | bytes 86024 | tf_op jit(solution)/shard_map/ppermute | solution.py:25
  5.9 1.3 collective-permute-start.16
  7.4 0.7 compare_select_fusion.3
  8.1 0.7 and_select_fusion.8
  10.4 1.2 collective-permute-start.1
  11.6 4.6 %collective-permute-done.1 = f32[8,256]{1,0:T(8,128)S(1)} collective-permute-done((f32[8,256]{1,0:T(8,128)S(1)}, f32[8,256]{1,0:T(8,128)S(1)}, u32[]{:S(2)}, u32[]{:S(2)}) %collective-permute-start.1) | collective-permute-done | bytes 8224 | tf_op jit(solution)/shard_map/ppermute | solution.py:94
  16.2 5.8 %collective-permute-done.2 = f32[8,256]{1,0:T(8,128)S(1)} collective-permute-done((f32[8,256]{1,0:T(8,128)S(1)}, f32[8,256]{1,0:T(8,128)S(1)}, u32[]{:S(2)}, u32[]{:S(2)}) %collective-permute-start.2) | collective-permute-done | bytes 8224 | tf_op jit(solution)/shard_map/ppermute | solution.py:94
  23.2 0.6 fusion.332
  24.4 0.6 fusion.250
  28.9 5.8 %collective-permute-done.4 = f32[8,256]{1,0:T(8,128)S(1)} collective-permute-done((f32[8,256]{1,0:T(8,128)S(1)}, f32[8,256]{1,0:T(8,128)S(1)}, u32[]{:S(2)}, u32[]{:S(2)}) %collective-permute-start.4) | collective-permute-done | bytes 8224 | tf_op jit(solution)/shard_map/ppermute | solution.py:94
  34.7 5.8 %collective-permute-done.5 = f32[8,256]{1,0:T(8,128)S(1)} collective-permute-done((f32[8,256]{1,0:T(8,128)S(1)}, f32[8,256]{1,0:T(8,128)S(1)}, u32[]{:S(2)}, u32[]{:S(2)}) %collective-permute-start.5) | collective-permute-done | bytes 8224 | tf_op jit(solution)/shard_map/ppermute | solution.py:94
  40.5 5.8 %collective-permute-done.6 = f32[8,256]{1,0:T(8,128)S(1)} collective-permute-done((f32[8,256]{1,0:T(8,128)S(1)}, f32[8,256]{1,0:T(8,128)S(1)}, u32[]{:S(2)}, u32[]{:S(2)}) %collective-permute-start.6) | collective-permute-done | bytes 8224 | tf_op jit(solution)/shard_map/ppermute | solution.py:94
  46.3 5.8 %collective-permute-done.7 = f32[8,256]{1,0:T(8,128)S(1)} collective-permute-done((f32[8,256]{1,0:T(8,128)S(1)}, f32[8,256]{1,0:T(8,128)S(1)}, u32[]{:S(2)}, u32[]{:S(2)}) %collective-permute-start.7) | collective-permute-done | bytes 8224 | tf_op jit(solution)/shard_map/ppermute | solution.py:94
  52.0 5.8 %collective-permute-done.8 = f32[8,256]{1,0:T(8,128)S(1)} collective-permute-done((f32[8,256]{1,0:T(8,128)S(1)}, f32[8,256]{1,0:T(8,128)S(1)}, u32[]{:S(2)}, u32[]{:S(2)}) %collective-permute-start.8) | collective-permute-done | bytes 8224 | tf_op jit(solution)/shard_map/ppermute | solution.py:94
  57.8 5.8 %collective-permute-done.9 = f32[8,256]{1,0:T(8,128)S(1)} collective-permute-done((f32[8,256]{1,0:T(8,128)S(1)}, f32[8,256]{1,0:T(8,128)S(1)}, u32[]{:S(2)}, u32[]{:S(2)}) %collective-permute-start.9) | collective-permute-done | bytes 8224 | tf_op jit(solution)/shard_map/ppermute | solution.py:94
  63.6 5.8 %collective-permute-done.10 = f32[8,256]{1,0:T(8,128)S(1)} collective-permute-done((f32[8,256]{1,0:T(8,128)S(1)}, f32[8,256]{1,0:T(8,128)S(1)}, u32[]{:S(2)}, u32[]{:S(2)}) %collective-permute-start.10) | collective-permute-done | bytes 8224 | tf_op jit(solution)/shard_map/ppermute | solution.py:94
  69.4 5.8 %collective-permute-done.11 = f32[8,256]{1,0:T(8,128)S(1)} collective-permute-done((f32[8,256]{1,0:T(8,128)S(1)}, f32[8,256]{1,0:T(8,128)S(1)}, u32[]{:S(2)}, u32[]{:S(2)}) %collective-permute-start.11) | collective-permute-done | bytes 8224 | tf_op jit(solution)/shard_map/ppermute | solution.py:94
  75.1 5.8 %collective-permute-done.12 = f32[8,256]{1,0:T(8,128)S(1)} collective-permute-done((f32[8,256]{1,0:T(8,128)S(1)}, f32[8,256]{1,0:T(8,128)S(1)}, u32[]{:S(2)}, u32[]{:S(2)}) %collective-permute-start.12) | collective-permute-done | bytes 8224 | tf_op jit(solution)/shard_map/ppermute | solution.py:94
  80.9 5.8 %collective-permute-done.13 = f32[8,256]{1,0:T(8,128)S(1)} collective-permute-done((f32[8,256]{1,0:T(8,128)S(1)}, f32[8,256]{1,0:T(8,128)S(1)}, u32[]{:S(2)}, u32[]{:S(2)}) %collective-permute-start.13) | collective-permute-done | bytes 8224 | tf_op jit(solution)/shard_map/ppermute | solution.py:94
  86.7 5.8 %collective-permute-done.14 = f32[8,256]{1,0:T(8,128)S(1)} collective-permute-done((f32[8,256]{1,0:T(8,128)S(1)}, f32[8,256]{1,0:T(8,128)S(1)}, u32[]{:S(2)}, u32[]{:S(2)}) %collective-permute-start.14) | collective-permute-done | bytes 8224 | tf_op jit(solution)/shard_map/ppermute | solution.py:94
  93.0 200.1 %gather_fusion.1 = f32[32768]{0:T(1024)S(1)} fusion(f32[8,4096]{1,0:T(8,128)S(1)} %gather_fusion, s32[32768]{0:T(1024)S(1)} %bitcast.250), kind=kCustom, calls=%fused_computation.1 | custom fusion | bytes 524288 | tf_op jit(solution)/shard_map/vmap()/gather | solution.py:49
  293.7 73.1 %while.12 = (s32[]{:T(128)}, f32[8,16,8,112]{3,2,1,0:T(8,128)S(1)}, f32[8,4096]{1,0:T(8,128)S(1)}, f32[32,24,128]{2,0,1:T(8,128)S(1)}, f32[32,24,128]{2,0,1:T(8,128)S(1)}, /*index=5*/s32[]{:T(128)}) while((s32[]{:T(128)}, f32[8,16,8,112]{3,2,1,0:T(8,128)S(1)}, f32[8,4096]{1,0:T(8,128)S(1)}, ...), condition=%wide.region_7.8_spmd.clone.clone, body=%wide.region_6.7_spmd.clone.clone.sunk | while | flops 234336256 | bytes 10379349 | solution.py:136
  297.9 0.7 multiply_subtract_fusion.2
  307.0 0.7 multiply_subtract_fusion.2
  316.1 0.7 multiply_subtract_fusion.2
  325.3 0.7 multiply_subtract_fusion.2
  334.4 0.7 multiply_subtract_fusion.2
  343.5 0.7 multiply_subtract_fusion.2
  352.7 0.7 multiply_subtract_fusion.2
  361.8 0.7 multiply_subtract_fusion.2
  367.0 0.8 divide_log_fusion
  (258 shorter events, 74.9 us)
Async XLA Ops:
  0.0 8.8 %copy-start.2 = (s32[6,3]{0,1:T(4,128)S(1)}, s32[6,3]{0,1:T(4,128)}, u32[]{:S(2)}) copy-start(s32[6,3]{0,1:T(4,128)} %constant.390.clone) | copy-start | bytes 220
  0.0 9.0 %copy-start.1 = (f32[8,256]{1,0:T(8,128)S(1)}, f32[8,256]{1,0:T(8,128)}, u32[]{:S(2)}) copy-start(f32[8,256]{1,0:T(8,128)} %param.9) | copy-start | bytes 24580
  0.0 10.4 %collective-permute-start = (f32[8,256]{1,0:T(8,128)}, f32[8,256]{1,0:T(8,128)S(1)}, u32[]{:S(2)}, u32[]{:S(2)}) collective-permute-start(f32[8,256]{1,0:T(8,128)} %param.9), channel_id=1, source_target_pairs={{0,1},{1,2},{2,3},{3,4},{4,5},{5,6},{6,7},{7,8},{8,9},{9,10},{10,1... | collective-permute-start | bytes 24584 | tf_op jit(solution)/shard_map/ppermute | solution.py:94
  1.3 20.7 %collective-permute-start.15 = (f32[8,8,112]{2,1,0:T(8,128)S(1)}, f32[8,8,112]{2,1,0:T(8,128)S(1)}, u32[]{:S(2)}, u32[]{:S(2)}) collective-permute-start(f32[8,8,112]{2,1,0:T(8,128)S(1)} %slice.34), channel_id=1, source_target_pairs={{0,1},{1,2},{2,3},{3,4},{4,5},{5,6},{6,7},{7,8},{8,9},{9,10},{10,1... | collective-permute-start | bytes 86024 | tf_op jit(solution)/shard_map/ppermute | solution.py:25
  5.9 16.1 %collective-permute-start.16 = (f32[8,8,112]{2,1,0:T(8,128)S(1)}, f32[8,8,112]{2,1,0:T(8,128)S(1)}, u32[]{:S(2)}, u32[]{:S(2)}) collective-permute-start(f32[8,8,112]{2,1,0:T(8,128)S(1)} %slice.36), channel_id=1, source_target_pairs={{1,0},{2,1},{3,2},{4,3},{5,4},{6,5},{7,6},{8,7},{9,8},{10,9},{11,1... | collective-permute-start | bytes 86024 | tf_op jit(solution)/shard_map/ppermute | solution.py:26
  9.1 0.8 copy-start
  9.3 0.8 copy-start.3
  10.4 5.8 %collective-permute-start.1 = (f32[8,256]{1,0:T(8,128)S(1)}, f32[8,256]{1,0:T(8,128)S(1)}, u32[]{:S(2)}, u32[]{:S(2)}) collective-permute-start(f32[8,256]{1,0:T(8,128)S(1)} %collective-permute-done), channel_id=1, source_target_pairs={{0,1},{1,2},{2,3},{3,4},{4,5},{5,6},{6,7},{7,8},{8,9},{9,10},{10,1... | collective-permute-start | bytes 24584 | tf_op jit(solution)/shard_map/ppermute | solution.py:94
  16.2 5.8 %collective-permute-start.2 = (f32[8,256]{1,0:T(8,128)S(1)}, f32[8,256]{1,0:T(8,128)S(1)}, u32[]{:S(2)}, u32[]{:S(2)}) collective-permute-start(f32[8,256]{1,0:T(8,128)S(1)} %collective-permute-done.1), channel_id=1, source_target_pairs={{0,1},{1,2},{2,3},{3,4},{4,5},{5,6},{6,7},{7,8},{8,9},{9,10},{10,1... | collective-permute-start | bytes 24584 | tf_op jit(solution)/shard_map/ppermute | solution.py:94
  22.0 6.9 %collective-permute-start.3 = (f32[8,256]{1,0:T(8,128)S(1)}, f32[8,256]{1,0:T(8,128)S(1)}, u32[]{:S(2)}, u32[]{:S(2)}) collective-permute-start(f32[8,256]{1,0:T(8,128)S(1)} %collective-permute-done.2), channel_id=1, source_target_pairs={{0,1},{1,2},{2,3},{3,4},{4,5},{5,6},{6,7},{7,8},{8,9},{9,10},{10,1... | collective-permute-start | bytes 24584 | tf_op jit(solution)/shard_map/ppermute | solution.py:94
  28.9 5.8 %collective-permute-start.4 = (f32[8,256]{1,0:T(8,128)S(1)}, f32[8,256]{1,0:T(8,128)S(1)}, u32[]{:S(2)}, u32[]{:S(2)}) collective-permute-start(f32[8,256]{1,0:T(8,128)S(1)} %collective-permute-done.3), channel_id=1, source_target_pairs={{0,1},{1,2},{2,3},{3,4},{4,5},{5,6},{6,7},{7,8},{8,9},{9,10},{10,1... | collective-permute-start | bytes 24584 | tf_op jit(solution)/shard_map/ppermute | solution.py:94
  34.7 5.8 %collective-permute-start.5 = (f32[8,256]{1,0:T(8,128)S(1)}, f32[8,256]{1,0:T(8,128)S(1)}, u32[]{:S(2)}, u32[]{:S(2)}) collective-permute-start(f32[8,256]{1,0:T(8,128)S(1)} %collective-permute-done.4), channel_id=1, source_target_pairs={{0,1},{1,2},{2,3},{3,4},{4,5},{5,6},{6,7},{7,8},{8,9},{9,10},{10,1... | collective-permute-start | bytes 24584 | tf_op jit(solution)/shard_map/ppermute | solution.py:94
  40.5 5.8 %collective-permute-start.6 = (f32[8,256]{1,0:T(8,128)S(1)}, f32[8,256]{1,0:T(8,128)S(1)}, u32[]{:S(2)}, u32[]{:S(2)}) collective-permute-start(f32[8,256]{1,0:T(8,128)S(1)} %collective-permute-done.5), channel_id=1, source_target_pairs={{0,1},{1,2},{2,3},{3,4},{4,5},{5,6},{6,7},{7,8},{8,9},{9,10},{10,1... | collective-permute-start | bytes 24584 | tf_op jit(solution)/shard_map/ppermute | solution.py:94
  46.3 5.8 %collective-permute-start.7 = (f32[8,256]{1,0:T(8,128)S(1)}, f32[8,256]{1,0:T(8,128)S(1)}, u32[]{:S(2)}, u32[]{:S(2)}) collective-permute-start(f32[8,256]{1,0:T(8,128)S(1)} %collective-permute-done.6), channel_id=1, source_target_pairs={{0,1},{1,2},{2,3},{3,4},{4,5},{5,6},{6,7},{7,8},{8,9},{9,10},{10,1... | collective-permute-start | bytes 24584 | tf_op jit(solution)/shard_map/ppermute | solution.py:94
  52.0 5.8 %collective-permute-start.8 = (f32[8,256]{1,0:T(8,128)S(1)}, f32[8,256]{1,0:T(8,128)S(1)}, u32[]{:S(2)}, u32[]{:S(2)}) collective-permute-start(f32[8,256]{1,0:T(8,128)S(1)} %collective-permute-done.7), channel_id=1, source_target_pairs={{0,1},{1,2},{2,3},{3,4},{4,5},{5,6},{6,7},{7,8},{8,9},{9,10},{10,1... | collective-permute-start | bytes 24584 | tf_op jit(solution)/shard_map/ppermute | solution.py:94
  57.8 5.8 %collective-permute-start.9 = (f32[8,256]{1,0:T(8,128)S(1)}, f32[8,256]{1,0:T(8,128)S(1)}, u32[]{:S(2)}, u32[]{:S(2)}) collective-permute-start(f32[8,256]{1,0:T(8,128)S(1)} %collective-permute-done.8), channel_id=1, source_target_pairs={{0,1},{1,2},{2,3},{3,4},{4,5},{5,6},{6,7},{7,8},{8,9},{9,10},{10,1... | collective-permute-start | bytes 24584 | tf_op jit(solution)/shard_map/ppermute | solution.py:94
  63.6 5.8 %collective-permute-start.10 = (f32[8,256]{1,0:T(8,128)S(1)}, f32[8,256]{1,0:T(8,128)S(1)}, u32[]{:S(2)}, u32[]{:S(2)}) collective-permute-start(f32[8,256]{1,0:T(8,128)S(1)} %collective-permute-done.9), channel_id=1, source_target_pairs={{0,1},{1,2},{2,3},{3,4},{4,5},{5,6},{6,7},{7,8},{8,9},{9,10},{10,1... | collective-permute-start | bytes 24584 | tf_op jit(solution)/shard_map/ppermute | solution.py:94
  69.3 5.8 %collective-permute-start.11 = (f32[8,256]{1,0:T(8,128)S(1)}, f32[8,256]{1,0:T(8,128)S(1)}, u32[]{:S(2)}, u32[]{:S(2)}) collective-permute-start(f32[8,256]{1,0:T(8,128)S(1)} %collective-permute-done.10), channel_id=1, source_target_pairs={{0,1},{1,2},{2,3},{3,4},{4,5},{5,6},{6,7},{7,8},{8,9},{9,10},{10,1... | collective-permute-start | bytes 24584 | tf_op jit(solution)/shard_map/ppermute | solution.py:94
  75.1 5.8 %collective-permute-start.12 = (f32[8,256]{1,0:T(8,128)S(1)}, f32[8,256]{1,0:T(8,128)S(1)}, u32[]{:S(2)}, u32[]{:S(2)}) collective-permute-start(f32[8,256]{1,0:T(8,128)S(1)} %collective-permute-done.11), channel_id=1, source_target_pairs={{0,1},{1,2},{2,3},{3,4},{4,5},{5,6},{6,7},{7,8},{8,9},{9,10},{10,1... | collective-permute-start | bytes 24584 | tf_op jit(solution)/shard_map/ppermute | solution.py:94
  80.9 5.8 %collective-permute-start.13 = (f32[8,256]{1,0:T(8,128)S(1)}, f32[8,256]{1,0:T(8,128)S(1)}, u32[]{:S(2)}, u32[]{:S(2)}) collective-permute-start(f32[8,256]{1,0:T(8,128)S(1)} %collective-permute-done.12), channel_id=1, source_target_pairs={{0,1},{1,2},{2,3},{3,4},{4,5},{5,6},{6,7},{7,8},{8,9},{9,10},{10,1... | collective-permute-start | bytes 24584 | tf_op jit(solution)/shard_map/ppermute | solution.py:94
  86.7 5.8 %collective-permute-start.14 = (f32[8,256]{1,0:T(8,128)S(1)}, f32[8,256]{1,0:T(8,128)S(1)}, u32[]{:S(2)}, u32[]{:S(2)}) collective-permute-start(f32[8,256]{1,0:T(8,128)S(1)} %collective-permute-done.13), channel_id=1, source_target_pairs={{0,1},{1,2},{2,3},{3,4},{4,5},{5,6},{6,7},{7,8},{8,9},{9,10},{10,1... | collective-permute-start | bytes 24584 | tf_op jit(solution)/shard_map/ppermute | solution.py:94
